TPU v7x, 512 devices: a whole 4x8x8 slice. The times are simulated.
512 devices in a mesh: grp: 16 (over x_lo, z), seq: 32 (over y, x_hi, core).
Axes of the slice: x: 4 (x_hi: 2, x_lo: 2; x = x_hi * 2 + x_lo), y: 8, z: 8, core: 2. Of those that a mesh axis runs over, the one named last changes fastest.
Arguments:
- signal: bfloat16 [131072, 256], P(('grp', 'seq')), may hold values from -6 to 6
- cotangent: bfloat16 [131072, 256], P(('grp', 'seq')), may hold values from -6 to 6
- w_taps: bfloat16 [512, 1024], replicated, may hold values from -0.25 to 0.25
- gate_bias: float32 [1024], replicated, may hold values from -3 to 3
- w_out: bfloat16 [512, 256], replicated, may hold values from -0.25 to 0.25
Outputs:
- block_out: bfloat16 [131072, 256], P(('grp', 'seq'))
- grad_in: bfloat16 [131072, 256], P(('grp', 'seq'))
- grad_taps: float32 [512, 1024], P('seq')
- grad_bias: float32 [1024], P('seq')
- grad_out: float32 [512, 256], P('seq')
All inputs are finite; a program needn't handle non-finite values.
Results may differ from a plain program's by a relative error of at most 0.0045.
Values may be sent and summed in bfloat16 or wider, within the bound.
No kernel may reach another device: no remote copies, remote signals or barrier semaphores. Data moves between devices by JAX's collectives and lax.ppermute only.
A program may use at most 64 MiB of HBM per device.

v0:
```python
import jax
import jax.numpy as jnp
from jax import lax
from jax.sharding import PartitionSpec as P


def from_behind(array, axis, by):
    count = lax.axis_size(axis)
    pairs = [(i, i + by) for i in range(count) if 0 <= i + by < count]
    return lax.ppermute(array, axis, pairs)


def reduced_row_axes(left, right):
    return lax.dot_general(
        left, right, (((0,), (0,)), ((), ())), preferred_element_type=jnp.float32
    )


def contract_cols(left, right):
    return lax.dot_general(
        left, right, (((1,), (1,)), ((), ())), preferred_element_type=jnp.float32
    )


def per_device(signal, cotangent, w_taps, gate_bias, w_out):
    width = signal.shape[1]
    units = w_out.shape[0]
    lagged_input = from_behind(signal, ("grp", "seq"), 2)
    preact = jnp.dot(signal, w_taps[width:], preferred_element_type=jnp.float32)
    preact = (
        preact
        + jnp.dot(lagged_input, w_taps[:width], preferred_element_type=jnp.float32)
        + gate_bias
    )
    squashed = jnp.tanh(preact[:, :units])
    opened = jax.nn.sigmoid(preact[:, units:])
    hidden_state = (squashed * opened).astype(jnp.bfloat16)
    block_out = (
        signal.astype(jnp.float32)
        + jnp.dot(hidden_state, w_out, preferred_element_type=jnp.float32)
    ).astype(jnp.bfloat16)
    grad_hidden = contract_cols(cotangent, w_out)
    grad_pre = jnp.concatenate(
        [
            grad_hidden * opened * (1.0 - squashed * squashed),
            grad_hidden * squashed * opened * (1.0 - opened),
        ],
        axis=1,
    ).astype(jnp.bfloat16)
    part_out = reduced_row_axes(hidden_state, cotangent)
    part_taps = jnp.concatenate(
        [reduced_row_axes(lagged_input, grad_pre), reduced_row_axes(signal, grad_pre)], axis=0
    )
    part_bias = jnp.sum(grad_pre.astype(jnp.float32), axis=0)
    later_pre = from_behind(grad_pre, ("grp", "seq"), -2)
    tapped_signal = contract_cols(later_pre, w_taps[:width])
    nearby = cotangent.astype(jnp.float32) + contract_cols(grad_pre, w_taps[width:])
    grad_in = (nearby + tapped_signal).astype(jnp.bfloat16)
    groups = lax.axis_size("seq")
    lanes = 128
    rows_taps = part_taps.shape[0] // groups
    rows_out = part_out.shape[0] // groups
    share_bias = part_bias.shape[0] // groups
    taps_r = rows_taps * part_taps.shape[1] // lanes
    out_r = rows_out * part_out.shape[1] // lanes
    bias_r = 8
    bias_rows = jnp.pad(
        part_bias.reshape(groups, 1, share_bias), ((0, 0), (0, bias_r), (0, lanes - share_bias))
    )[:, :bias_r]
    packed = jnp.concatenate(
        [
            part_taps.reshape(groups, taps_r, lanes),
            part_out.reshape(groups, out_r, lanes),
            bias_rows,
        ],
        axis=1,
    ).reshape(groups * (taps_r + out_r + bias_r), lanes)
    mine = lax.psum_scatter(packed, "seq", scatter_dimension=0, tiled=True)
    mine = lax.psum(mine, "grp")
    grad_taps = mine[:taps_r].reshape(rows_taps, part_taps.shape[1])
    grad_out = mine[taps_r : taps_r + out_r].reshape(rows_out, part_out.shape[1])
    grad_bias = mine[taps_r + out_r, :share_bias]
    return (block_out, grad_in, grad_taps, grad_bias, grad_out)


def solution(mesh):
    placed = (P(("grp", "seq"), None), P(("grp", "seq"), None), P(), P(), P())
    return jax.shard_map(
        per_device,
        mesh=mesh,
        in_specs=placed,
        out_specs=(
            P(("grp", "seq"), None),
            P(("grp", "seq"), None),
            P("seq", None),
            P("seq"),
            P("seq", None),
        ),
        check_vma=False,
    )
```

profile of v0, /device:TPU:6, one launch (start us, length us, event | category | flops | bytes accessed | tf_op | source)
XLA Modules:
  0.0 307.3 jit_solution(14182650442721048356)
XLA Ops:
  7.2 0.0 copy-start
  7.2 0.0 reduce-scatter.4.cloned.1.call-start
  7.2 4.5 %collective-permute-start = (bf16[256,256]{1,0:T(8,128)(2,1)}, bf16[256,256]{1,0:T(8,128)(2,1)S(1)}, u32[]{:S(2)}, u32[]{:S(2)}) collective-permute-start(bf16[256,256]{1,0:T(8,128)(2,1)} %param.5), channel_id=1, source_target_pairs={{0,2},{1,3},{2,4},{3,5},{4,6},{5,7},{6,8},{7,9},{8,10},{9,11},{10,... | collective-permute-start | bytes 393224 | tf_op jit(solution)/shard_map/ppermute | solution.py:10
  11.7 1.4 fusion.9
  13.1 3.1 %collective-permute-done = bf16[256,256]{1,0:T(8,128)(2,1)S(1)} collective-permute-done((bf16[256,256]{1,0:T(8,128)(2,1)}, bf16[256,256]{1,0:T(8,128)(2,1)S(1)}, u32[]{:S(2)}, u32[]{:S(2)}) %collective-permute-start) | collective-permute-done | bytes 131104 | tf_op jit(solution)/shard_map/ppermute | solution.py:10
  16.2 1.3 fusion
  17.6 0.4 multiply_convert_fusion.1
  18.1 0.1 convert_reduce_fusion
  18.2 0.3 copy-done.2
  18.5 0.3 convolution_bitcast_fusion
  18.8 0.1 reshape.31
  18.9 0.7 pad_slice_fusion
  19.6 0.3 fusion.11
  19.9 0.3 convolution_bitcast_fusion.1
  20.3 1.5 pad_maximum_fusion.1
  21.7 1.7 reshape.29
  23.5 2.6 pad_maximum_fusion
  26.1 0.0 reduce-scatter.4.cloned.1.call-update
  26.1 0.0 all-reduce.4.cloned.1.call-start
  26.2 0.1 pad_maximum_fusion.2
  26.3 13.1 %collective-permute-start.1 = (bf16[256,1024]{1,0:T(8,128)(2,1)S(1)}, bf16[256,1024]{1,0:T(8,128)(2,1)S(1)}, u32[]{:S(2)}, u32[]{:S(2)}) collective-permute-start(bf16[256,1024]{1,0:T(8,128)(2,1)S(1)} %pad_maximum_fusion.2), channel_id=1, source_target_pairs={{2,0},{3,1},{4,2},{5,3},{6,4},{7,5},{8,6},{9,7},{10,8},{11,9},{12,... | collective-permute-start | bytes 1572872 | tf_op jit(solution)/shard_map/ppermute | solution.py:10
  39.4 0.9 fusion.1
  40.2 0.3 convolution_add_fusion.3
  40.6 116.4 %reduce-scatter.4.cloned.1.call-done = f32[168,128]{1,0:T(8,128)} async-done(((f32[5376,128]{1,0:T(8,128)}), f32[168,128]{1,0:T(8,128)}) %reduce-scatter.4.cloned.1.call-update) | async-done | bytes 86032
  157.0 0.0 all-reduce.4.cloned.1.call-update
  157.1 1.0 fusion.2
  158.1 138.4 %all-reduce.4.cloned.1.call-done = f32[168,128]{1,0:T(8,128)} async-done(((f32[168,128]{1,0:T(8,128)}), f32[168,128]{1,0:T(8,128)}) %all-reduce.4.cloned.1.call-update) | async-done | bytes 86032 | tf_op jit(solution)/shard_map/psum | solution.py:79
  296.5 0.8 slice.36
  297.3 0.6 reshape.33
  298.0 0.7 slice.38
  298.7 0.6 reshape.34
  299.3 1.2 slice_bitcast_fusion
  (14 shorter events, 0.1 us)
Async XLA Ops:
  7.2 10.4 %copy-start = (bf16[512,256]{1,0:T(8,128)(2,1)S(1)}, bf16[512,256]{1,0:T(8,128)(2,1)}, u32[]{:S(2)}) copy-start(bf16[512,256]{1,0:T(8,128)(2,1)} %param.9) | copy-start | bytes 786436
  7.2 10.4 %copy-start.5 = (bf16[256,256]{1,0:T(8,128)(2,1)S(1)}, bf16[256,256]{1,0:T(8,128)(2,1)}, u32[]{:S(2)}) copy-start(bf16[256,256]{1,0:T(8,128)(2,1)} %param.6) | copy-start | bytes 393220
  7.2 149.8 %reduce-scatter.4.cloned.1.call-start = ((), (), s32[]{:S(2)}) async-start(), calls=%async_computation.2 | async-start | bytes 2838528
  7.2 9.0 %collective-permute-start = (bf16[256,256]{1,0:T(8,128)(2,1)}, bf16[256,256]{1,0:T(8,128)(2,1)S(1)}, u32[]{:S(2)}, u32[]{:S(2)}) collective-permute-start(bf16[256,256]{1,0:T(8,128)(2,1)} %param.5), channel_id=1, source_target_pairs={{0,2},{1,3},{2,4},{3,5},{4,6},{5,7},{6,8},{7,9},{8,10},{9,11},{10,... | collective-permute-start | bytes 393224 | tf_op jit(solution)/shard_map/ppermute | solution.py:10
  17.6 0.9 copy-start.2
  18.1 2.2 copy-start.3
  26.1 13.2 %copy-start.4 = (bf16[256,512]{1,0:T(8,128)(2,1)S(1)}, bf16[256,512]{1,0:T(8,128)(2,1)}, u32[]{:S(2)}) copy-start(bf16[256,512]{1,0:T(8,128)(2,1)} %copy-done.3) | copy-start | bytes 786436
  26.1 14.1 %copy-start.1 = (bf16[512,1024]{1,0:T(8,128)(2,1)S(1)}, bf16[512,1024]{1,0:T(8,128)(2,1)}, u32[]{:S(2)}) copy-start(bf16[512,1024]{1,0:T(8,128)(2,1)} %param.7) | copy-start | bytes 3145732
  26.1 14.1 %copy-start.6 = (bf16[256,256]{1,0:T(8,128)(2,1)S(1)}, bf16[256,256]{1,0:T(8,128)(2,1)}, u32[]{:S(2)}) copy-start(bf16[256,256]{1,0:T(8,128)(2,1)} %param.6) | copy-start | bytes 393220
  26.1 270.3 %all-reduce.4.cloned.1.call-start = ((), (), s32[]{:S(2)}) async-start(), calls=%async_computation.1 | async-start | bytes 172032 | tf_op jit(solution)/shard_map/psum | solution.py:79
  26.3 130.8 %collective-permute-start.1 = (bf16[256,1024]{1,0:T(8,128)(2,1)S(1)}, bf16[256,1024]{1,0:T(8,128)(2,1)S(1)}, u32[]{:S(2)}, u32[]{:S(2)}) collective-permute-start(bf16[256,1024]{1,0:T(8,128)(2,1)S(1)} %pad_maximum_fusion.2), channel_id=1, source_target_pairs={{2,0},{3,1},{4,2},{5,3},{6,4},{7,5},{8,6},{9,7},{10,8},{11,9},{12,... | collective-permute-start | bytes 1572872 | tf_op jit(solution)/shard_map/ppermute | solution.py:10
Sparse Core Ops, SparseCore 0:
  26.3 130.7 reduce-scatter.3
  159.9 136.4 all-reduce.3
where the time goes:
time: 308 us; the launch traced here: 307 us
  waiting for transfers between devices  258 us (84%)
  starting transfers between devices  17.6 us (6%)
  between operations  14.2 us (5%)
  local copies, waits for them, and re-layouts  6.88 us (2%)
  matrix products  6.37 us (2%)
  other arithmetic  4.29 us (1%)
    psum x1, waiting for transfers between devices, per_device(): mine = lax.psum(mine, 'grp')  138 us
    unnamed x3, waiting for transfers between devices  116 us
    ppermute x2, starting transfers between devices, from_behind(): return lax.ppermute(array, axis, pairs)  17.5 us
  transfers between devices with their start and end apart: 4, of which 3 were waited for; matrix products, arithmetic and copies ran while one was open for 1% of the time, Pallas kernels for 0%

commit v1 on v0

--- a/solution.py
+++ b/solution.py
@@ -76,7 +76,7 @@
         axis=1,
     ).reshape(groups * (taps_r + out_r + bias_r), lanes)
     mine = lax.psum_scatter(packed, "seq", scatter_dimension=0, tiled=True)
-    mine = lax.psum(mine, "grp")
+    mine = jnp.sum(lax.all_gather(mine, "grp"), axis=0)
     grad_taps = mine[:taps_r].reshape(rows_taps, part_taps.shape[1])
     grad_out = mine[taps_r : taps_r + out_r].reshape(rows_out, part_out.shape[1])
     grad_bias = mine[taps_r + out_r, :share_bias]

time: 308 us -> 242 us (0.79)
  waiting for transfers between devices: 258 us -> 202 us
  starting transfers between devices: 17.6 us -> 8.3 us
    psum x1 -> x0, waiting for transfers between devices: 138 us -> none  [per_device(): mine = lax.psum(mine, 'grp')]
    all_gather x0 -> x1, waiting for transfers between devices: none -> 59.5 us  [per_device(): mine = jnp.sum(lax.all_gather(mine, 'grp'), axis=0)]
    unnamed x3, waiting for transfers between devices: 116 us -> 131 us
    ppermute x2, starting transfers between devices: 17.5 us -> 8.22 us  [from_behind(): return lax.ppermute(array, axis, pairs)]
    ppermute x2, waiting for transfers between devices: 3.09 us -> 11.5 us  [from_behind(): return lax.ppermute(array, axis, pairs)]
  transfers between devices with their start and end apart: 4 -> 4, of which waited for: 3 -> 4; matrix products, arithmetic and copies ran while one was open for 1% -> 2% of each run, Pallas kernels for 0% -> 0%
where the time goes in v1:
time: 242 us; the launch traced here: 241 us
  waiting for transfers between devices  202 us (83%)
  between operations  14.2 us (6%)
  starting transfers between devices  8.3 us (3%)
  matrix products  6.36 us (3%)
  other arithmetic  5.7 us (2%)
  local copies, waits for them, and re-layouts  4.65 us (2%)
    unnamed x3, waiting for transfers between devices  131 us
    all_gather x1, waiting for transfers between devices, per_device(): mine = jnp.sum(lax.all_gather(mine, 'grp'), axis=0)  59.5 us
    ppermute x2, waiting for transfers between devices, from_behind(): return lax.ppermute(array, axis, pairs)  11.5 us
    ppermute x2, starting transfers between devices, from_behind(): return lax.ppermute(array, axis, pairs)  8.22 us
  transfers between devices with their start and end apart: 4, of which 4 were waited for; matrix products, arithmetic and copies ran while one was open for 2% of the time, Pallas kernels for 0%

profile of v1, /device:TPU:6, one launch (start us, length us, event | category | flops | bytes accessed | tf_op | source)
XLA Modules:
  0.0 241.3 jit_solution(12903264072030874815)
XLA Ops:
  7.2 0.0 copy-start
  7.2 0.0 reduce-scatter.4.cloned.1.call-start
  7.2 4.5 %collective-permute-start = (bf16[256,256]{1,0:T(8,128)(2,1)}, bf16[256,256]{1,0:T(8,128)(2,1)S(1)}, u32[]{:S(2)}, u32[]{:S(2)}) collective-permute-start(bf16[256,256]{1,0:T(8,128)(2,1)} %param.5), channel_id=1, source_target_pairs={{0,2},{1,3},{2,4},{3,5},{4,6},{5,7},{6,8},{7,9},{8,10},{9,11},{10,... | collective-permute-start | bytes 393224 | tf_op jit(solution)/shard_map/ppermute | solution.py:10
  11.7 1.4 fusion.9
  13.1 3.1 %collective-permute-done = bf16[256,256]{1,0:T(8,128)(2,1)S(1)} collective-permute-done((bf16[256,256]{1,0:T(8,128)(2,1)}, bf16[256,256]{1,0:T(8,128)(2,1)S(1)}, u32[]{:S(2)}, u32[]{:S(2)}) %collective-permute-start) | collective-permute-done | bytes 131104 | tf_op jit(solution)/shard_map/ppermute | solution.py:10
  16.2 1.3 fusion
  17.6 0.4 multiply_convert_fusion.1
  18.1 0.1 convert_reduce_fusion
  18.2 0.3 copy-done.2
  18.5 0.3 convolution_bitcast_fusion
  18.8 0.1 reshape.31
  18.9 0.7 pad_slice_fusion
  19.6 0.3 fusion.11
  19.9 0.3 convolution_bitcast_fusion.1
  20.3 1.5 pad_maximum_fusion.1
  21.7 1.7 reshape.29
  23.5 2.6 %pad_maximum_fusion = f32[32,168,128]{2,1,0:T(8,128)} fusion(f32[32,8,128]{2,1,0:T(8,128)} %pad_slice_fusion, f32[32,32,128]{2,1,0:T(8,128)S(1)} %reshape.30, f32[32,128,128]{2,1,0:T(8,128)S(1)} %reshape.29), kind=kLoop, calls=%fused_computation | loop fusion | flops 1376256 | bytes 5505024 | tf_op jit(solution)/shard_map/concatenate | solution.py:70
  26.1 0.0 reduce-scatter.4.cloned.1.call-update
  26.1 0.0 all-gather.3.cloned.1.call-start
  26.2 131.0 %reduce-scatter.4.cloned.1.call-done = f32[168,128]{1,0:T(8,128)} async-done(((f32[5376,128]{1,0:T(8,128)}), f32[168,128]{1,0:T(8,128)}) %reduce-scatter.4.cloned.1.call-update) | async-done | bytes 86032
  157.2 0.0 all-gather.3.cloned.1.call-update
  157.2 0.1 pad_maximum_fusion.2
  157.3 3.8 %collective-permute-start.1 = (bf16[256,1024]{1,0:T(8,128)(2,1)S(1)}, bf16[256,1024]{1,0:T(8,128)(2,1)S(1)}, u32[]{:S(2)}, u32[]{:S(2)}) collective-permute-start(bf16[256,1024]{1,0:T(8,128)(2,1)S(1)} %pad_maximum_fusion.2), channel_id=1, source_target_pairs={{2,0},{3,1},{4,2},{5,3},{6,4},{7,5},{8,6},{9,7},{10,8},{11,9},{12,... | collective-permute-start | bytes 1572872 | tf_op jit(solution)/shard_map/ppermute | solution.py:10
  161.1 0.9 fusion.1
  161.9 0.3 convolution_add_fusion.3
  162.3 8.5 %collective-permute-done.1 = bf16[256,1024]{1,0:T(8,128)(2,1)S(1)} collective-permute-done((bf16[256,1024]{1,0:T(8,128)(2,1)S(1)}, bf16[256,1024]{1,0:T(8,128)(2,1)S(1)}, u32[]{:S(2)}, u32[]{:S(2)}) %collective-permute-start.1) | collective-permute-done | bytes 524320 | tf_op jit(solution)/shard_map/ppermute | solution.py:10
  170.7 1.0 fusion.2
  171.7 59.5 %all-gather.3.cloned.1.call-done = f32[2688,128]{1,0:T(8,128)} async-done(((f32[168,128]{1,0:T(8,128)}), f32[2688,128]{1,0:T(8,128)}) %all-gather.3.cloned.1.call-update) | async-done | bytes 1376272 | tf_op jit(solution)/shard_map/all_gather | solution.py:79
  231.2 1.4 reduce_sum.19
  232.6 0.5 slice_bitcast_fusion
  233.2 0.6 reshape.33
  233.8 0.6 reshape.34
  (15 shorter events, 0.1 us)
Async XLA Ops:
  7.2 10.4 %copy-start = (bf16[512,256]{1,0:T(8,128)(2,1)S(1)}, bf16[512,256]{1,0:T(8,128)(2,1)}, u32[]{:S(2)}) copy-start(bf16[512,256]{1,0:T(8,128)(2,1)} %param.9) | copy-start | bytes 786436
  7.2 10.4 %copy-start.5 = (bf16[256,256]{1,0:T(8,128)(2,1)S(1)}, bf16[256,256]{1,0:T(8,128)(2,1)}, u32[]{:S(2)}) copy-start(bf16[256,256]{1,0:T(8,128)(2,1)} %param.6) | copy-start | bytes 393220
  7.2 150.0 %reduce-scatter.4.cloned.1.call-start = ((), (), s32[]{:S(2)}) async-start(), calls=%async_computation.2 | async-start | bytes 2838528
  7.2 9.0 %collective-permute-start = (bf16[256,256]{1,0:T(8,128)(2,1)}, bf16[256,256]{1,0:T(8,128)(2,1)S(1)}, u32[]{:S(2)}, u32[]{:S(2)}) collective-permute-start(bf16[256,256]{1,0:T(8,128)(2,1)} %param.5), channel_id=1, source_target_pairs={{0,2},{1,3},{2,4},{3,5},{4,6},{5,7},{6,8},{7,9},{8,10},{9,11},{10,... | collective-permute-start | bytes 393224 | tf_op jit(solution)/shard_map/ppermute | solution.py:10
  17.6 0.9 copy-start.2
  18.1 1.8 copy-start.3
  26.1 134.9 %copy-start.4 = (bf16[256,512]{1,0:T(8,128)(2,1)S(1)}, bf16[256,512]{1,0:T(8,128)(2,1)}, u32[]{:S(2)}) copy-start(bf16[256,512]{1,0:T(8,128)(2,1)} %copy-done.3) | copy-start | bytes 786436
  26.1 135.8 %copy-start.1 = (bf16[512,1024]{1,0:T(8,128)(2,1)S(1)}, bf16[512,1024]{1,0:T(8,128)(2,1)}, u32[]{:S(2)}) copy-start(bf16[512,1024]{1,0:T(8,128)(2,1)} %param.7) | copy-start | bytes 3145732
  26.1 135.8 %copy-start.6 = (bf16[256,256]{1,0:T(8,128)(2,1)S(1)}, bf16[256,256]{1,0:T(8,128)(2,1)}, u32[]{:S(2)}) copy-start(bf16[256,256]{1,0:T(8,128)(2,1)} %param.6) | copy-start | bytes 393220
  26.1 205.1 %all-gather.3.cloned.1.call-start = ((), (), s32[]{:S(2)}) async-start(), calls=%async_computation.1 | async-start | bytes 1462272 | tf_op jit(solution)/shard_map/all_gather | solution.py:79
  157.3 13.5 %collective-permute-start.1 = (bf16[256,1024]{1,0:T(8,128)(2,1)S(1)}, bf16[256,1024]{1,0:T(8,128)(2,1)S(1)}, u32[]{:S(2)}, u32[]{:S(2)}) collective-permute-start(bf16[256,1024]{1,0:T(8,128)(2,1)S(1)} %pad_maximum_fusion.2), channel_id=1, source_target_pairs={{2,0},{3,1},{4,2},{5,3},{6,4},{7,5},{8,6},{9,7},{10,8},{11,9},{12,... | collective-permute-start | bytes 1572872 | tf_op jit(solution)/shard_map/ppermute | solution.py:10
Sparse Core Ops, SparseCore 0:
  26.3 130.8 reduce-scatter.3
  159.3 71.9 all-gather.2
